TPU v7x, 32 devices: a whole 2x2x4 slice. The times are simulated.
32 devices in a mesh: outer: 4 (over z), inner: 8 (over y, x, core).
Axes of the slice: x: 2, y: 2, z: 4, core: 2. Of those that a mesh axis runs over, the one named last changes fastest.
Arguments:
- queries: bfloat16 [8192, 1024], P(('outer', 'inner')), may hold values from -60 to 60
- key_states: bfloat16 [8192, 128], P(('outer', 'inner')), may hold values from -6 to 6
- value_states: bfloat16 [8192, 128], P(('outer', 'inner')), may hold values from -6 to 6
- grad_output: bfloat16 [8192, 1024], P(('outer', 'inner')), may hold values from -6 to 6
- documents: int32 [8192], replicated, may hold values from 0 to 20, never falling along the last dimension, each value on 1 to 768 neighbouring positions
- block_order: int32 [64], replicated, may hold values from 0 to 63, as said below
Outputs:
- grad_queries: bfloat16 [8192, 1024], P(('outer', 'inner'))
- grad_keys: bfloat16 [8192, 128], P(('outer', 'inner'))
- grad_values: bfloat16 [8192, 128], P(('outer', 'inner'))
Inputs may be any that keep to these rules, and one draw needn't show every extreme that they name: `documents`: never falling along the sequence; every document has 1 to 768 positions and one has exactly 768. `block_order`: device d of the joined index outer, inner (d = outer * 8 + inner) holds stored blocks 2 * d and 2 * d + 1, which are sequence blocks d and 63 - d in either order.
All inputs are finite; a program needn't handle non-finite values.
Results may differ from a plain program's by a relative error of at most 0.0049.
Values may be sent and summed in bfloat16 or wider, within the bound.
No kernel may reach another device: no remote copies, remote signals or barrier semaphores. Data moves between devices by JAX's collectives and lax.ppermute only.
A program may use at most 64 MiB of HBM per device.

v0:
```python
import math

import jax
import jax.numpy as jnp
from jax import lax
from jax.sharding import PartitionSpec as P

REACH = 6


NEGATIVE = -1e30


def padded(block, sides, width):
    for axis, dim in sides:
        count = lax.axis_size(axis)
        forward = [(i, i + 1) for i in range(count - 1)]
        backward = [(target, source) for source, target in forward]
        low = lax.ppermute(
            lax.slice_in_dim(block, block.shape[dim] - width, None, axis=dim), axis, forward
        )
        high = lax.ppermute(lax.slice_in_dim(block, 0, width, axis=dim), axis, backward)
        block = jnp.concatenate([low, block, high], axis=dim)
    return block


def stack_two(first_item, second_item):
    return jnp.stack([first_item, second_item])


def take_block(block_rows, slot_index, length):
    return lax.dynamic_slice_in_dim(block_rows, slot_index * length, length, 0)


def split_heads(block_rows, head_size):
    return block_rows.reshape(block_rows.shape[0], block_rows.shape[1] // head_size, head_size)


def allowed_pairs(documents, query_block, key_block, length):
    offsets = jnp.arange(length, dtype=jnp.int32)
    query_place = query_block * length + offsets
    key_place = key_block * length + offsets
    query_owner = lax.dynamic_slice_in_dim(documents, query_block * length, length, 0)
    key_owner = lax.dynamic_slice_in_dim(documents, jnp.maximum(key_block, 0) * length, length, 0)
    same_owner = key_owner[None, :] == query_owner[:, None]
    return (key_block >= 0) & (key_place[None, :] <= query_place[:, None]) & same_owner


def forward_blocks(extended, first_block, length, at_top):
    from_above = extended[extended.shape[0] - length :]
    return (extended[:length], jnp.where(at_top, first_block, from_above))


def send_back(carried, length, at_top, stashed=None):
    extended = padded(
        jnp.concatenate([carried[0], carried[1]], 0), ((("outer", "inner"), 0),), length
    )
    new_second = extended[:length]
    new_first = jnp.where(at_top, carried[1], extended[extended.shape[0] - length :])
    return stack_two(new_first, new_second)


def apply_pairs(update, allowed_sets, operands):
    return jax.vmap(update)(allowed_sets, *operands)


def on_device(queries, key_states, value_states, grad_output, documents, block_order):
    axis_count = lax.axis_size(("outer", "inner"))
    device = lax.axis_index(("outer", "inner"))
    length = key_states.shape[0] // 2
    head_size = key_states.shape[1]
    factor = 1.0 / math.sqrt(head_size)
    slot_zero = block_order[2 * device]
    slot_one = block_order[2 * device + 1]
    first_slot = jnp.where(slot_zero < axis_count, 0, 1).astype(jnp.int32)
    second_slot = 1 - first_slot
    first_block = jnp.minimum(slot_zero, slot_one)
    second_block = jnp.maximum(slot_zero, slot_one)
    at_top = device == axis_count - 1
    joined = jnp.concatenate([key_states, value_states], 1)
    moving = (take_block(joined, first_slot, length), take_block(joined, second_slot, length))
    query_pair = stack_two(
        split_heads(take_block(queries, first_slot, length), head_size),
        split_heads(take_block(queries, second_slot, length), head_size),
    )
    output_pair = stack_two(
        split_heads(take_block(grad_output, first_slot, length), head_size),
        split_heads(take_block(grad_output, second_slot, length), head_size),
    )
    head_count = query_pair.shape[2]

    def pair_scores(query_heads, output_heads, pair_blocks):
        key_part = pair_blocks[:, :head_size]
        value_part = pair_blocks[:, head_size:]
        scores = (
            jnp.einsum("bhd,wd->hbw", query_heads, key_part, preferred_element_type=jnp.float32)
            * factor
        )
        grad_prob = jnp.einsum(
            "bhd,wd->hbw", output_heads, value_part, preferred_element_type=jnp.float32
        )
        return (scores, grad_prob)

    def stats_update(
        allowed, running_max, totals, weighted, query_heads, output_heads, pair_blocks
    ):
        scores, grad_prob = pair_scores(query_heads, output_heads, pair_blocks)
        masked = jnp.where(allowed[None], scores, NEGATIVE)
        new_max = jnp.maximum(running_max, masked.max(-1))
        rescale = jnp.exp(running_max - new_max)
        weights = jnp.where(allowed[None], jnp.exp(scores - new_max[..., None]), 0.0)
        return (
            new_max,
            totals * rescale + weights.sum(-1),
            weighted * rescale + (weights * grad_prob).sum(-1),
        )

    def grad_update(allowed, query_heads, output_heads, pair_blocks, log_totals, row_dots):
        scores, grad_prob = pair_scores(query_heads, output_heads, pair_blocks)
        probabilities = jnp.where(allowed[None], jnp.exp(scores - log_totals[..., None]), 0.0)
        grad_scores = probabilities * (grad_prob - row_dots[..., None])
        rounded_probs = probabilities.astype(jnp.bfloat16)
        rounded_grads = grad_scores.astype(jnp.bfloat16)
        grad_rows = jnp.einsum(
            "hbw,wd->bhd",
            rounded_grads,
            pair_blocks[:, :head_size],
            preferred_element_type=jnp.float32,
        )
        grad_key = jnp.einsum(
            "hbw,bhd->wd", rounded_grads, query_heads, preferred_element_type=jnp.float32
        )
        grad_value = jnp.einsum(
            "hbw,bhd->wd", rounded_probs, output_heads, preferred_element_type=jnp.float32
        )
        return (grad_rows, jnp.concatenate([grad_key, grad_value], 1))

    def pair_masks(offset):
        return stack_two(
            allowed_pairs(documents, first_block, first_block - offset, length),
            allowed_pairs(documents, second_block, second_block - offset, length),
        )

    blank_stats = jnp.zeros((2, head_count, length), jnp.float32)
    running = (jnp.full((2, head_count, length), NEGATIVE, jnp.float32), blank_stats, blank_stats)
    received = []
    for offset in range(REACH + 1):
        if offset > 0:
            extended = padded(
                jnp.concatenate([moving[1], moving[0]], 0), ((("outer", "inner"), 0),), length
            )
            moving = forward_blocks(extended, moving[0], length, at_top)
        received.append(stack_two(moving[0], moving[1]))
        running = apply_pairs(
            stats_update, pair_masks(offset), running + (query_pair, output_pair, received[offset])
        )
    log_totals = running[0] + jnp.log(running[1])
    row_dots = running[2] / running[1]
    shared = (query_pair, output_pair)
    grad_total = jnp.zeros(query_pair.shape, jnp.float32)
    for offset in range(REACH, -1, -1):
        grad_part, contribution = apply_pairs(
            grad_update, pair_masks(offset), shared + (received[offset], log_totals, row_dots)
        )
        grad_total = grad_total + grad_part
        carried = (
            contribution if offset == REACH else send_back(carried, length, at_top) + contribution
        )
    grad_query = (
        (grad_total * factor).astype(jnp.bfloat16).reshape(2, length, head_count * head_size)
    )
    grad_key = (carried[:, :, :head_size] * factor).astype(jnp.bfloat16)
    grad_value = carried[:, :, head_size:].astype(jnp.bfloat16)

    def restore(paired):
        return jnp.concatenate([paired[first_slot], paired[second_slot]], 0)

    return (restore(grad_query), restore(grad_key), restore(grad_value))


def solution(mesh):
    in_specs = (
        P(("outer", "inner"), None),
        P(("outer", "inner"), None),
        P(("outer", "inner"), None),
        P(("outer", "inner"), None),
        P(),
        P(),
    )
    out_specs = (
        P(("outer", "inner"), None),
        P(("outer", "inner"), None),
        P(("outer", "inner"), None),
    )
    return jax.shard_map(
        on_device, mesh=mesh, in_specs=in_specs, out_specs=out_specs, check_vma=False
    )
```

profile of v0, /device:TPU:8, one launch (start us, length us, event | category | flops | bytes accessed | tf_op | source)
XLA Modules:
  0.0 149.3 jit_solution(10851049472074881526)
XLA Ops:
  4.4 3.7 %collective-permute-start.6 = (bf16[128,256]{1,0:T(8,128)(2,1)S(1)}, bf16[128,256]{1,0:T(8,128)(2,1)S(1)}, u32[]{:S(2)}, u32[]{:S(2)}) collective-permute-start(bf16[128,256]{1,0:T(8,128)(2,1)S(1)} %constant_dynamic-slice_fusion.6), channel_id=1, source_target_pairs={{1,0},{2,1},{3,2},{4,3},{5,4},{6,5},{7,6},{8,7},{9,8},{10,9},{11,1... | collective-permute-start | bytes 196616 | tf_op jit(solution)/shard_map/ppermute | solution.py:22
  17.6 5.4 %collective-permute-start.7 = (bf16[128,256]{1,0:T(8,128)(2,1)S(1)}, bf16[128,256]{1,0:T(8,128)(2,1)S(1)}, u32[]{:S(2)}, u32[]{:S(2)}) collective-permute-start(bf16[128,256]{1,0:T(8,128)(2,1)S(1)} %get-tuple-element.27), channel_id=1, source_target_pairs={{1,0},{2,1},{3,2},{4,3},{5,4},{6,5},{7,6},{8,7},{9,8},{10,9},{11,1... | collective-permute-start | bytes 196616 | tf_op jit(solution)/shard_map/ppermute | solution.py:22
  24.9 5.5 %collective-permute-start.8 = (bf16[128,256]{1,0:T(8,128)(2,1)S(1)}, bf16[128,256]{1,0:T(8,128)(2,1)S(1)}, u32[]{:S(2)}, u32[]{:S(2)}) collective-permute-start(bf16[128,256]{1,0:T(8,128)(2,1)S(1)} %broadcast_select_fusion.3), channel_id=1, source_target_pairs={{1,0},{2,1},{3,2},{4,3},{5,4},{6,5},{7,6},{8,7},{9,8},{10,9},{11,1... | collective-permute-start | bytes 196616 | tf_op jit(solution)/shard_map/ppermute | solution.py:22
  32.7 5.2 %collective-permute-done.1 = bf16[128,256]{1,0:T(8,128)(2,1)S(1)} collective-permute-done((bf16[128,256]{1,0:T(8,128)(2,1)S(1)}, bf16[128,256]{1,0:T(8,128)(2,1)S(1)}, u32[]{:S(2)}, u32[]{:S(2)}) %collective-permute-start.1) | collective-permute-done | bytes 65568 | tf_op jit(solution)/shard_map/ppermute | solution.py:19
  39.8 2.4 %collective-permute-start.2 = (bf16[128,256]{1,0:T(8,128)(2,1)S(1)}, bf16[128,256]{1,0:T(8,128)(2,1)S(1)}, u32[]{:S(2)}, u32[]{:S(2)}) collective-permute-start(bf16[128,256]{1,0:T(8,128)(2,1)S(1)} %collective-permute-done.1), channel_id=1, source_target_pairs={{0,1},{1,2},{2,3},{3,4},{4,5},{5,6},{6,7},{7,8},{8,9},{9,10},{10,1... | collective-permute-start | bytes 196616 | tf_op jit(solution)/shard_map/ppermute | solution.py:19
  42.6 4.7 %collective-permute-done.2 = bf16[128,256]{1,0:T(8,128)(2,1)S(1)} collective-permute-done((bf16[128,256]{1,0:T(8,128)(2,1)S(1)}, bf16[128,256]{1,0:T(8,128)(2,1)S(1)}, u32[]{:S(2)}, u32[]{:S(2)}) %collective-permute-start.2) | collective-permute-done | bytes 65568 | tf_op jit(solution)/shard_map/ppermute | solution.py:19
  49.2 2.4 %collective-permute-start.3 = (bf16[128,256]{1,0:T(8,128)(2,1)S(1)}, bf16[128,256]{1,0:T(8,128)(2,1)S(1)}, u32[]{:S(2)}, u32[]{:S(2)}) collective-permute-start(bf16[128,256]{1,0:T(8,128)(2,1)S(1)} %collective-permute-done.2), channel_id=1, source_target_pairs={{0,1},{1,2},{2,3},{3,4},{4,5},{5,6},{6,7},{7,8},{8,9},{9,10},{10,1... | collective-permute-start | bytes 196616 | tf_op jit(solution)/shard_map/ppermute | solution.py:19
  52.0 4.7 %collective-permute-done.3 = bf16[128,256]{1,0:T(8,128)(2,1)S(1)} collective-permute-done((bf16[128,256]{1,0:T(8,128)(2,1)S(1)}, bf16[128,256]{1,0:T(8,128)(2,1)S(1)}, u32[]{:S(2)}, u32[]{:S(2)}) %collective-permute-start.3) | collective-permute-done | bytes 65568 | tf_op jit(solution)/shard_map/ppermute | solution.py:19
  58.7 2.4 %collective-permute-start.4 = (bf16[128,256]{1,0:T(8,128)(2,1)S(1)}, bf16[128,256]{1,0:T(8,128)(2,1)S(1)}, u32[]{:S(2)}, u32[]{:S(2)}) collective-permute-start(bf16[128,256]{1,0:T(8,128)(2,1)S(1)} %collective-permute-done.3), channel_id=1, source_target_pairs={{0,1},{1,2},{2,3},{3,4},{4,5},{5,6},{6,7},{7,8},{8,9},{9,10},{10,1... | collective-permute-start | bytes 196616 | tf_op jit(solution)/shard_map/ppermute | solution.py:19
  61.4 4.6 %collective-permute-done.4 = bf16[128,256]{1,0:T(8,128)(2,1)S(1)} collective-permute-done((bf16[128,256]{1,0:T(8,128)(2,1)S(1)}, bf16[128,256]{1,0:T(8,128)(2,1)S(1)}, u32[]{:S(2)}, u32[]{:S(2)}) %collective-permute-start.4) | collective-permute-done | bytes 65568 | tf_op jit(solution)/shard_map/ppermute | solution.py:19
  68.3 5.4 %collective-permute-done.5 = bf16[128,256]{1,0:T(8,128)(2,1)S(1)} collective-permute-done((bf16[128,256]{1,0:T(8,128)(2,1)S(1)}, bf16[128,256]{1,0:T(8,128)(2,1)S(1)}, u32[]{:S(2)}, u32[]{:S(2)}) %collective-permute-start.5) | collective-permute-done | bytes 65568 | tf_op jit(solution)/shard_map/ppermute | solution.py:19
  80.6 2.1 %collective-permute-start.12 = (f32[128,256]{1,0:T(8,128)S(1)}, f32[128,256]{1,0:T(8,128)S(1)}, u32[]{:S(2)}, u32[]{:S(2)}) collective-permute-start(f32[128,256]{1,0:T(8,128)S(1)} %fusion.54), channel_id=1, source_target_pairs={{1,0},{2,1},{3,2},{4,3},{5,4},{6,5},{7,6},{8,7},{9,8},{10,9},{11,1... | collective-permute-start | bytes 393224 | tf_op jit(solution)/shard_map/ppermute | solution.py:22
  86.7 2.4 %collective-permute-start.13 = (f32[128,256]{1,0:T(8,128)S(1)}, f32[128,256]{1,0:T(8,128)S(1)}, u32[]{:S(2)}, u32[]{:S(2)}) collective-permute-start(f32[128,256]{1,0:T(8,128)S(1)} %get-tuple-element.18), channel_id=1, source_target_pairs={{0,1},{1,2},{2,3},{3,4},{4,5},{5,6},{6,7},{7,8},{8,9},{9,10},{10,1... | collective-permute-start | bytes 393224 | tf_op jit(solution)/shard_map/ppermute | solution.py:19
  89.4 5.4 %collective-permute-done.13 = f32[128,256]{1,0:T(8,128)S(1)} collective-permute-done((f32[128,256]{1,0:T(8,128)S(1)}, f32[128,256]{1,0:T(8,128)S(1)}, u32[]{:S(2)}, u32[]{:S(2)}) %collective-permute-start.13) | collective-permute-done | bytes 131104 | tf_op jit(solution)/shard_map/ppermute | solution.py:19
  97.1 2.4 %collective-permute-start.15 = (f32[128,256]{1,0:T(8,128)S(1)}, f32[128,256]{1,0:T(8,128)S(1)}, u32[]{:S(2)}, u32[]{:S(2)}) collective-permute-start(f32[128,256]{1,0:T(8,128)S(1)} %get-tuple-element.44), channel_id=1, source_target_pairs={{0,1},{1,2},{2,3},{3,4},{4,5},{5,6},{6,7},{7,8},{8,9},{9,10},{10,1... | collective-permute-start | bytes 393224 | tf_op jit(solution)/shard_map/ppermute | solution.py:19
  99.5 5.7 %collective-permute-done.15 = f32[128,256]{1,0:T(8,128)S(1)} collective-permute-done((f32[128,256]{1,0:T(8,128)S(1)}, f32[128,256]{1,0:T(8,128)S(1)}, u32[]{:S(2)}, u32[]{:S(2)}) %collective-permute-start.15) | collective-permute-done | bytes 131104 | tf_op jit(solution)/shard_map/ppermute | solution.py:19
  107.5 2.4 %collective-permute-start.17 = (f32[128,256]{1,0:T(8,128)S(1)}, f32[128,256]{1,0:T(8,128)S(1)}, u32[]{:S(2)}, u32[]{:S(2)}) collective-permute-start(f32[128,256]{1,0:T(8,128)S(1)} %get-tuple-element.42), channel_id=1, source_target_pairs={{0,1},{1,2},{2,3},{3,4},{4,5},{5,6},{6,7},{7,8},{8,9},{9,10},{10,1... | collective-permute-start | bytes 393224 | tf_op jit(solution)/shard_map/ppermute | solution.py:19
  110.0 5.7 %collective-permute-done.17 = f32[128,256]{1,0:T(8,128)S(1)} collective-permute-done((f32[128,256]{1,0:T(8,128)S(1)}, f32[128,256]{1,0:T(8,128)S(1)}, u32[]{:S(2)}, u32[]{:S(2)}) %collective-permute-start.17) | collective-permute-done | bytes 131104 | tf_op jit(solution)/shard_map/ppermute | solution.py:19
  118.0 2.4 %collective-permute-start.19 = (f32[128,256]{1,0:T(8,128)S(1)}, f32[128,256]{1,0:T(8,128)S(1)}, u32[]{:S(2)}, u32[]{:S(2)}) collective-permute-start(f32[128,256]{1,0:T(8,128)S(1)} %get-tuple-element.40), channel_id=1, source_target_pairs={{0,1},{1,2},{2,3},{3,4},{4,5},{5,6},{6,7},{7,8},{8,9},{9,10},{10,1... | collective-permute-start | bytes 393224 | tf_op jit(solution)/shard_map/ppermute | solution.py:19
  120.5 5.7 %collective-permute-done.19 = f32[128,256]{1,0:T(8,128)S(1)} collective-permute-done((f32[128,256]{1,0:T(8,128)S(1)}, f32[128,256]{1,0:T(8,128)S(1)}, u32[]{:S(2)}, u32[]{:S(2)}) %collective-permute-start.19) | collective-permute-done | bytes 131104 | tf_op jit(solution)/shard_map/ppermute | solution.py:19
  128.5 2.4 %collective-permute-start.21 = (f32[128,256]{1,0:T(8,128)S(1)}, f32[128,256]{1,0:T(8,128)S(1)}, u32[]{:S(2)}, u32[]{:S(2)}) collective-permute-start(f32[128,256]{1,0:T(8,128)S(1)} %get-tuple-element.38), channel_id=1, source_target_pairs={{0,1},{1,2},{2,3},{3,4},{4,5},{5,6},{6,7},{7,8},{8,9},{9,10},{10,1... | collective-permute-start | bytes 393224 | tf_op jit(solution)/shard_map/ppermute | solution.py:19
  130.9 5.7 %collective-permute-done.21 = f32[128,256]{1,0:T(8,128)S(1)} collective-permute-done((f32[128,256]{1,0:T(8,128)S(1)}, f32[128,256]{1,0:T(8,128)S(1)}, u32[]{:S(2)}, u32[]{:S(2)}) %collective-permute-start.21) | collective-permute-done | bytes 131104 | tf_op jit(solution)/shard_map/ppermute | solution.py:19
  139.8 2.4 %collective-permute-start.23 = (f32[128,256]{1,0:T(8,128)S(1)}, f32[128,256]{1,0:T(8,128)S(1)}, u32[]{:S(2)}, u32[]{:S(2)}) collective-permute-start(f32[128,256]{1,0:T(8,128)S(1)} %get-tuple-element.36), channel_id=1, source_target_pairs={{0,1},{1,2},{2,3},{3,4},{4,5},{5,6},{6,7},{7,8},{8,9},{9,10},{10,1... | collective-permute-start | bytes 393224 | tf_op jit(solution)/shard_map/ppermute | solution.py:19
  142.3 5.6 %collective-permute-done.23 = f32[128,256]{1,0:T(8,128)S(1)} collective-permute-done((f32[128,256]{1,0:T(8,128)S(1)}, f32[128,256]{1,0:T(8,128)S(1)}, u32[]{:S(2)}, u32[]{:S(2)}) %collective-permute-start.23) | collective-permute-done | bytes 131104 | tf_op jit(solution)/shard_map/ppermute | solution.py:19
  (135 shorter events, 47.1 us)
Async XLA Ops:
  4.4 11.2 %collective-permute-start.6 = (bf16[128,256]{1,0:T(8,128)(2,1)S(1)}, bf16[128,256]{1,0:T(8,128)(2,1)S(1)}, u32[]{:S(2)}, u32[]{:S(2)}) collective-permute-start(bf16[128,256]{1,0:T(8,128)(2,1)S(1)} %constant_dynamic-slice_fusion.6), channel_id=1, source_target_pairs={{1,0},{2,1},{3,2},{4,3},{5,4},{6,5},{7,6},{8,7},{9,8},{10,9},{11,1... | collective-permute-start | bytes 196616 | tf_op jit(solution)/shard_map/ppermute | solution.py:22
  15.7 7.7 %collective-permute-start = (bf16[128,256]{1,0:T(8,128)(2,1)S(1)}, bf16[128,256]{1,0:T(8,128)(2,1)S(1)}, u32[]{:S(2)}, u32[]{:S(2)}) collective-permute-start(bf16[128,256]{1,0:T(8,128)(2,1)S(1)} %get-tuple-element.28), channel_id=1, source_target_pairs={{0,1},{1,2},{2,3},{3,4},{4,5},{5,6},{6,7},{7,8},{8,9},{9,10},{10,1... | collective-permute-start | bytes 196616 | tf_op jit(solution)/shard_map/ppermute | solution.py:19
  17.6 7.3 %collective-permute-start.7 = (bf16[128,256]{1,0:T(8,128)(2,1)S(1)}, bf16[128,256]{1,0:T(8,128)(2,1)S(1)}, u32[]{:S(2)}, u32[]{:S(2)}) collective-permute-start(bf16[128,256]{1,0:T(8,128)(2,1)S(1)} %get-tuple-element.27), channel_id=1, source_target_pairs={{1,0},{2,1},{3,2},{4,3},{5,4},{6,5},{7,6},{8,7},{9,8},{10,9},{11,1... | collective-permute-start | bytes 196616 | tf_op jit(solution)/shard_map/ppermute | solution.py:22
  24.9 7.8 %collective-permute-start.8 = (bf16[128,256]{1,0:T(8,128)(2,1)S(1)}, bf16[128,256]{1,0:T(8,128)(2,1)S(1)}, u32[]{:S(2)}, u32[]{:S(2)}) collective-permute-start(bf16[128,256]{1,0:T(8,128)(2,1)S(1)} %broadcast_select_fusion.3), channel_id=1, source_target_pairs={{1,0},{2,1},{3,2},{4,3},{5,4},{6,5},{7,6},{8,7},{9,8},{10,9},{11,1... | collective-permute-start | bytes 196616 | tf_op jit(solution)/shard_map/ppermute | solution.py:22
  30.4 7.4 %collective-permute-start.1 = (bf16[128,256]{1,0:T(8,128)(2,1)S(1)}, bf16[128,256]{1,0:T(8,128)(2,1)S(1)}, u32[]{:S(2)}, u32[]{:S(2)}) collective-permute-start(bf16[128,256]{1,0:T(8,128)(2,1)S(1)} %collective-permute-done), channel_id=1, source_target_pairs={{0,1},{1,2},{2,3},{3,4},{4,5},{5,6},{6,7},{7,8},{8,9},{9,10},{10,1... | collective-permute-start | bytes 196616 | tf_op jit(solution)/shard_map/ppermute | solution.py:19
  37.9 9.4 %collective-permute-start.9 = (bf16[128,256]{1,0:T(8,128)(2,1)S(1)}, bf16[128,256]{1,0:T(8,128)(2,1)S(1)}, u32[]{:S(2)}, u32[]{:S(2)}) collective-permute-start(bf16[128,256]{1,0:T(8,128)(2,1)S(1)} %broadcast_select_fusion.2), channel_id=1, source_target_pairs={{1,0},{2,1},{3,2},{4,3},{5,4},{6,5},{7,6},{8,7},{9,8},{10,9},{11,1... | collective-permute-start | bytes 196616 | tf_op jit(solution)/shard_map/ppermute | solution.py:22
  39.8 7.5 %collective-permute-start.2 = (bf16[128,256]{1,0:T(8,128)(2,1)S(1)}, bf16[128,256]{1,0:T(8,128)(2,1)S(1)}, u32[]{:S(2)}, u32[]{:S(2)}) collective-permute-start(bf16[128,256]{1,0:T(8,128)(2,1)S(1)} %collective-permute-done.1), channel_id=1, source_target_pairs={{0,1},{1,2},{2,3},{3,4},{4,5},{5,6},{6,7},{7,8},{8,9},{9,10},{10,1... | collective-permute-start | bytes 196616 | tf_op jit(solution)/shard_map/ppermute | solution.py:19
  47.3 9.4 %collective-permute-start.10 = (bf16[128,256]{1,0:T(8,128)(2,1)S(1)}, bf16[128,256]{1,0:T(8,128)(2,1)S(1)}, u32[]{:S(2)}, u32[]{:S(2)}) collective-permute-start(bf16[128,256]{1,0:T(8,128)(2,1)S(1)} %broadcast_select_fusion.1), channel_id=1, source_target_pairs={{1,0},{2,1},{3,2},{4,3},{5,4},{6,5},{7,6},{8,7},{9,8},{10,9},{11,1... | collective-permute-start | bytes 196616 | tf_op jit(solution)/shard_map/ppermute | solution.py:22
  49.2 7.5 %collective-permute-start.3 = (bf16[128,256]{1,0:T(8,128)(2,1)S(1)}, bf16[128,256]{1,0:T(8,128)(2,1)S(1)}, u32[]{:S(2)}, u32[]{:S(2)}) collective-permute-start(bf16[128,256]{1,0:T(8,128)(2,1)S(1)} %collective-permute-done.2), channel_id=1, source_target_pairs={{0,1},{1,2},{2,3},{3,4},{4,5},{5,6},{6,7},{7,8},{8,9},{9,10},{10,1... | collective-permute-start | bytes 196616 | tf_op jit(solution)/shard_map/ppermute | solution.py:19
  56.7 11.6 %collective-permute-start.11 = (bf16[128,256]{1,0:T(8,128)(2,1)S(1)}, bf16[128,256]{1,0:T(8,128)(2,1)S(1)}, u32[]{:S(2)}, u32[]{:S(2)}) collective-permute-start(bf16[128,256]{1,0:T(8,128)(2,1)S(1)} %broadcast_select_fusion), channel_id=1, source_target_pairs={{1,0},{2,1},{3,2},{4,3},{5,4},{6,5},{7,6},{8,7},{9,8},{10,9},{11,1... | collective-permute-start | bytes 196616 | tf_op jit(solution)/shard_map/ppermute | solution.py:22
  58.7 7.4 %collective-permute-start.4 = (bf16[128,256]{1,0:T(8,128)(2,1)S(1)}, bf16[128,256]{1,0:T(8,128)(2,1)S(1)}, u32[]{:S(2)}, u32[]{:S(2)}) collective-permute-start(bf16[128,256]{1,0:T(8,128)(2,1)S(1)} %collective-permute-done.3), channel_id=1, source_target_pairs={{0,1},{1,2},{2,3},{3,4},{4,5},{5,6},{6,7},{7,8},{8,9},{9,10},{10,1... | collective-permute-start | bytes 196616 | tf_op jit(solution)/shard_map/ppermute | solution.py:19
  66.4 7.4 %collective-permute-start.5 = (bf16[128,256]{1,0:T(8,128)(2,1)S(1)}, bf16[128,256]{1,0:T(8,128)(2,1)S(1)}, u32[]{:S(2)}, u32[]{:S(2)}) collective-permute-start(bf16[128,256]{1,0:T(8,128)(2,1)S(1)} %collective-permute-done.4), channel_id=1, source_target_pairs={{0,1},{1,2},{2,3},{3,4},{4,5},{5,6},{6,7},{7,8},{8,9},{9,10},{10,1... | collective-permute-start | bytes 196616 | tf_op jit(solution)/shard_map/ppermute | solution.py:19
  80.6 6.1 %collective-permute-start.12 = (f32[128,256]{1,0:T(8,128)S(1)}, f32[128,256]{1,0:T(8,128)S(1)}, u32[]{:S(2)}, u32[]{:S(2)}) collective-permute-start(f32[128,256]{1,0:T(8,128)S(1)} %fusion.54), channel_id=1, source_target_pairs={{1,0},{2,1},{3,2},{4,3},{5,4},{6,5},{7,6},{8,7},{9,8},{10,9},{11,1... | collective-permute-start | bytes 393224 | tf_op jit(solution)/shard_map/ppermute | solution.py:22
  86.7 8.1 %collective-permute-start.13 = (f32[128,256]{1,0:T(8,128)S(1)}, f32[128,256]{1,0:T(8,128)S(1)}, u32[]{:S(2)}, u32[]{:S(2)}) collective-permute-start(f32[128,256]{1,0:T(8,128)S(1)} %get-tuple-element.18), channel_id=1, source_target_pairs={{0,1},{1,2},{2,3},{3,4},{4,5},{5,6},{6,7},{7,8},{8,9},{9,10},{10,1... | collective-permute-start | bytes 393224 | tf_op jit(solution)/shard_map/ppermute | solution.py:19
  94.8 4.6 %collective-permute-start.14 = (f32[128,256]{1,0:T(8,128)S(1)}, f32[128,256]{1,0:T(8,128)S(1)}, u32[]{:S(2)}, u32[]{:S(2)}) collective-permute-start(f32[128,256]{1,0:T(8,128)S(1)} %get-tuple-element.43), channel_id=1, source_target_pairs={{1,0},{2,1},{3,2},{4,3},{5,4},{6,5},{7,6},{8,7},{9,8},{10,9},{11,1... | collective-permute-start | bytes 393224 | tf_op jit(solution)/shard_map/ppermute | solution.py:22
  97.1 8.2 %collective-permute-start.15 = (f32[128,256]{1,0:T(8,128)S(1)}, f32[128,256]{1,0:T(8,128)S(1)}, u32[]{:S(2)}, u32[]{:S(2)}) collective-permute-start(f32[128,256]{1,0:T(8,128)S(1)} %get-tuple-element.44), channel_id=1, source_target_pairs={{0,1},{1,2},{2,3},{3,4},{4,5},{5,6},{6,7},{7,8},{8,9},{9,10},{10,1... | collective-permute-start | bytes 393224 | tf_op jit(solution)/shard_map/ppermute | solution.py:19
  105.3 4.6 %collective-permute-start.16 = (f32[128,256]{1,0:T(8,128)S(1)}, f32[128,256]{1,0:T(8,128)S(1)}, u32[]{:S(2)}, u32[]{:S(2)}) collective-permute-start(f32[128,256]{1,0:T(8,128)S(1)} %get-tuple-element.41), channel_id=1, source_target_pairs={{1,0},{2,1},{3,2},{4,3},{5,4},{6,5},{7,6},{8,7},{9,8},{10,9},{11,1... | collective-permute-start | bytes 393224 | tf_op jit(solution)/shard_map/ppermute | solution.py:22
  107.5 8.2 %collective-permute-start.17 = (f32[128,256]{1,0:T(8,128)S(1)}, f32[128,256]{1,0:T(8,128)S(1)}, u32[]{:S(2)}, u32[]{:S(2)}) collective-permute-start(f32[128,256]{1,0:T(8,128)S(1)} %get-tuple-element.42), channel_id=1, source_target_pairs={{0,1},{1,2},{2,3},{3,4},{4,5},{5,6},{6,7},{7,8},{8,9},{9,10},{10,1... | collective-permute-start | bytes 393224 | tf_op jit(solution)/shard_map/ppermute | solution.py:19
  115.8 4.6 %collective-permute-start.18 = (f32[128,256]{1,0:T(8,128)S(1)}, f32[128,256]{1,0:T(8,128)S(1)}, u32[]{:S(2)}, u32[]{:S(2)}) collective-permute-start(f32[128,256]{1,0:T(8,128)S(1)} %get-tuple-element.39), channel_id=1, source_target_pairs={{1,0},{2,1},{3,2},{4,3},{5,4},{6,5},{7,6},{8,7},{9,8},{10,9},{11,1... | collective-permute-start | bytes 393224 | tf_op jit(solution)/shard_map/ppermute | solution.py:22
  118.0 8.2 %collective-permute-start.19 = (f32[128,256]{1,0:T(8,128)S(1)}, f32[128,256]{1,0:T(8,128)S(1)}, u32[]{:S(2)}, u32[]{:S(2)}) collective-permute-start(f32[128,256]{1,0:T(8,128)S(1)} %get-tuple-element.40), channel_id=1, source_target_pairs={{0,1},{1,2},{2,3},{3,4},{4,5},{5,6},{6,7},{7,8},{8,9},{9,10},{10,1... | collective-permute-start | bytes 393224 | tf_op jit(solution)/shard_map/ppermute | solution.py:19
  126.3 4.6 %collective-permute-start.20 = (f32[128,256]{1,0:T(8,128)S(1)}, f32[128,256]{1,0:T(8,128)S(1)}, u32[]{:S(2)}, u32[]{:S(2)}) collective-permute-start(f32[128,256]{1,0:T(8,128)S(1)} %get-tuple-element.37), channel_id=1, source_target_pairs={{1,0},{2,1},{3,2},{4,3},{5,4},{6,5},{7,6},{8,7},{9,8},{10,9},{11,1... | collective-permute-start | bytes 393224 | tf_op jit(solution)/shard_map/ppermute | solution.py:22
  128.5 8.2 %collective-permute-start.21 = (f32[128,256]{1,0:T(8,128)S(1)}, f32[128,256]{1,0:T(8,128)S(1)}, u32[]{:S(2)}, u32[]{:S(2)}) collective-permute-start(f32[128,256]{1,0:T(8,128)S(1)} %get-tuple-element.38), channel_id=1, source_target_pairs={{0,1},{1,2},{2,3},{3,4},{4,5},{5,6},{6,7},{7,8},{8,9},{9,10},{10,1... | collective-permute-start | bytes 393224 | tf_op jit(solution)/shard_map/ppermute | solution.py:19
  136.7 5.5 %collective-permute-start.22 = (f32[128,256]{1,0:T(8,128)S(1)}, f32[128,256]{1,0:T(8,128)S(1)}, u32[]{:S(2)}, u32[]{:S(2)}) collective-permute-start(f32[128,256]{1,0:T(8,128)S(1)} %get-tuple-element.35), channel_id=1, source_target_pairs={{1,0},{2,1},{3,2},{4,3},{5,4},{6,5},{7,6},{8,7},{9,8},{10,9},{11,1... | collective-permute-start | bytes 393224 | tf_op jit(solution)/shard_map/ppermute | solution.py:22
  139.8 8.1 %collective-permute-start.23 = (f32[128,256]{1,0:T(8,128)S(1)}, f32[128,256]{1,0:T(8,128)S(1)}, u32[]{:S(2)}, u32[]{:S(2)}) collective-permute-start(f32[128,256]{1,0:T(8,128)S(1)} %get-tuple-element.36), channel_id=1, source_target_pairs={{0,1},{1,2},{2,3},{3,4},{4,5},{5,6},{6,7},{7,8},{8,9},{9,10},{10,1... | collective-permute-start | bytes 393224 | tf_op jit(solution)/shard_map/ppermute | solution.py:19
  (1 other events, 10.3 us)
where the time goes:
time: 150 us; the launch traced here: 149 us
  waiting for transfers between devices  60.2 us (40%)
  starting transfers between devices  59.5 us (40%)
  matrix products  11.7 us (8%)
  local copies, waits for them, and re-layouts  7.2 us (5%)
  other arithmetic  5.48 us (4%)
  between operations  5.17 us (3%)
    ppermute x12, waiting for transfers between devices, padded(): lax.ppermute(lax.slice_in_dim(block, block.shape[dim] - width, None, axis...  58.7 us
    ppermute x12, starting transfers between devices, padded(): lax.ppermute(lax.slice_in_dim(block, 0, width, axis=dim), axis, backward)  32.1 us
    ppermute x12, starting transfers between devices, padded(): lax.ppermute(lax.slice_in_dim(block, block.shape[dim] - width, None, axis...  27.4 us
  transfers between devices with their start and end apart: 24, of which 12 were waited for; matrix products, arithmetic and copies ran while one was open for 9% of the time, Pallas kernels for 0%

commit v1 on v0

v1 whole, which is shorter than its diff:
```python
import math

import jax
import jax.numpy as jnp
import numpy as np
from jax import lax
from jax.sharding import PartitionSpec as P

REACH = 6

NEGATIVE = -1e30

AXES = ("outer", "inner")


def slot_tables(count):
    slots = 2 + 3 * REACH
    place = np.full((count, slots), -1, np.int64)
    for d in range(count):
        place[d, 0] = d
        place[d, 1] = 2 * count - 1 - d
        for k in range(1, REACH + 1):
            if d - k >= 0:
                place[d, 2 + k - 1] = d - k
            if d + k <= count - 1:
                place[d, 2 + REACH + 2 * (k - 1)] = d + k
                place[d, 3 + REACH + 2 * (k - 1)] = 2 * count - 1 - d - k
    window = np.zeros((count, 2, REACH + 1), np.int32)
    key_block = np.full((count, 2, REACH + 1), -1, np.int32)
    sources = np.full((count, slots, 2), 2 * (REACH + 1), np.int32)
    for d in range(count):
        filled = np.zeros(slots, np.int64)
        for q, query_block in enumerate((d, 2 * count - 1 - d)):
            for k in range(REACH + 1):
                target = query_block - (REACH - k)
                found = np.nonzero(place[d] == target)[0] if target >= 0 else []
                if len(found) == 0:
                    assert target < 0
                    continue
                m = int(found[0])
                window[d, q, k] = m
                key_block[d, q, k] = target
                sources[d, m, filled[m]] = q * (REACH + 1) + k
                filled[m] += 1
    return window, key_block, sources


def on_device(queries, key_states, value_states, grad_output, documents, block_order):
    count = lax.axis_size(AXES)
    device = lax.axis_index(AXES)
    length = key_states.shape[0] // 2
    head_size = key_states.shape[1]
    factor = 1.0 / math.sqrt(head_size)
    span = REACH + 1
    window_np, key_block_np, sources_np = slot_tables(count)

    first_slot = jnp.where(block_order[2 * device] < count, 0, 1).astype(jnp.int32)
    second_slot = 1 - first_slot

    def take_block(rows, slot):
        return lax.dynamic_slice_in_dim(rows, slot * length, length, 0)

    joined = jnp.concatenate([key_states, value_states], 1)
    low = take_block(joined, first_slot)
    high = take_block(joined, second_slot)
    both = jnp.concatenate([low, high], 0)

    received_low = []
    received_both = []
    for k in range(1, REACH + 1):
        up = [(s, s + k) for s in range(count - k)]
        down = [(s, s - k) for s in range(k, count)]
        received_low.append(lax.ppermute(low, AXES, up))
        received_both.append(lax.ppermute(both, AXES, down))
    held = [low, high] + received_low
    for pair in received_both:
        held += [pair[:length], pair[length:]]
    held = jnp.stack(held)

    window_idx = jnp.asarray(window_np)[device].reshape(-1)
    key_blocks = jnp.asarray(key_block_np)[device]
    windows = jnp.take(held, window_idx, axis=0).reshape(2, span * length, 2 * head_size)
    key_window = windows[..., :head_size]
    value_window = windows[..., head_size:]

    def split_heads(rows):
        return rows.reshape(rows.shape[0], rows.shape[1] // head_size, head_size)

    query_pair = jnp.stack(
        [split_heads(take_block(queries, first_slot)), split_heads(take_block(queries, second_slot))]
    )
    output_pair = jnp.stack(
        [
            split_heads(take_block(grad_output, first_slot)),
            split_heads(take_block(grad_output, second_slot)),
        ]
    )

    query_blocks = jnp.stack([device, 2 * count - 1 - device])
    offsets = jnp.arange(length, dtype=jnp.int32)
    query_place = query_blocks[:, None] * length + offsets[None, :]
    key_place = (key_blocks[:, :, None] * length + offsets[None, None, :]).reshape(2, span * length)
    query_owner = jnp.take(documents, query_place)
    key_owner = jnp.take(documents, jnp.maximum(key_place, 0))
    allowed = (
        (key_place[:, None, :] >= 0)
        & (key_place[:, None, :] <= query_place[:, :, None])
        & (key_owner[:, None, :] == query_owner[:, :, None])
    )[:, None]

    scores = (
        jnp.einsum("qbhd,qwd->qhbw", query_pair, key_window, preferred_element_type=jnp.float32)
        * factor
    )
    grad_prob = jnp.einsum(
        "qbhd,qwd->qhbw", output_pair, value_window, preferred_element_type=jnp.float32
    )
    masked = jnp.where(allowed, scores, NEGATIVE)
    top = masked.max(-1)
    weights = jnp.where(allowed, jnp.exp(scores - top[..., None]), 0.0)
    log_totals = top + jnp.log(weights.sum(-1))
    probabilities = jnp.where(allowed, jnp.exp(scores - log_totals[..., None]), 0.0)
    row_dots = (probabilities * grad_prob).sum(-1)
    grad_scores = probabilities * (grad_prob - row_dots[..., None])
    rounded_probs = probabilities.astype(jnp.bfloat16)
    rounded_grads = grad_scores.astype(jnp.bfloat16)

    grad_query = jnp.einsum(
        "qhbw,qwd->qbhd", rounded_grads, key_window, preferred_element_type=jnp.float32
    )
    grad_key = jnp.einsum(
        "qhbw,qbhd->qwd", rounded_grads, query_pair, preferred_element_type=jnp.float32
    )
    grad_value = jnp.einsum(
        "qhbw,qbhd->qwd", rounded_probs, output_pair, preferred_element_type=jnp.float32
    )
    parts = jnp.concatenate([grad_key, grad_value], -1).reshape(2 * span, length, 2 * head_size)
    parts = jnp.concatenate([parts, jnp.zeros((1,) + parts.shape[1:], parts.dtype)], 0)
    sources = jnp.asarray(sources_np)[device]
    summed = jnp.take(parts, sources[:, 0], axis=0) + jnp.take(parts, sources[:, 1], axis=0)

    grad_low = summed[0]
    grad_high = summed[1]
    for k in range(1, REACH + 1):
        up = [(s + k, s) for s in range(count - k)]
        down = [(s - k, s) for s in range(k, count)]
        grad_low = grad_low + lax.ppermute(summed[2 + k - 1], AXES, up)
        back = lax.ppermute(
            jnp.concatenate(
                [summed[2 + REACH + 2 * (k - 1)], summed[3 + REACH + 2 * (k - 1)]], 0
            ),
            AXES,
            down,
        )
        grad_low = grad_low + back[:length]
        grad_high = grad_high + back[length:]

    grad_query = (
        (grad_query * factor).astype(jnp.bfloat16).reshape(2, length, query_pair.shape[2] * head_size)
    )
    grad_kv = jnp.stack([grad_low, grad_high])
    grad_keys = (grad_kv[:, :, :head_size] * factor).astype(jnp.bfloat16)
    grad_values = grad_kv[:, :, head_size:].astype(jnp.bfloat16)

    def restore(paired):
        return jnp.concatenate([paired[first_slot], paired[second_slot]], 0)

    return (restore(grad_query), restore(grad_keys), restore(grad_values))


def solution(mesh):
    in_specs = (
        P(AXES, None),
        P(AXES, None),
        P(AXES, None),
        P(AXES, None),
        P(),
        P(),
    )
    out_specs = (
        P(AXES, None),
        P(AXES, None),
        P(AXES, None),
    )
    return jax.shard_map(
        on_device, mesh=mesh, in_specs=in_specs, out_specs=out_specs, check_vma=False
    )
```

time: 150 us -> 153 us (1.020)
  the two profiles are of different devices: /device:TPU:8 before, /device:TPU:20 now
where the time goes in v1:
time: 153 us; the launch traced here: 152 us
  starting transfers between devices  80 us (52%)
  local copies, waits for them, and re-layouts  31.2 us (20%)
  other arithmetic  19.1 us (12%)
  waiting for transfers between devices  12.4 us (8%)
  matrix products  6.94 us (5%)
  between operations  2.19 us (1%)
    ppermute x6, starting transfers between devices, on_device(): grad_low = grad_low + lax.ppermute(summed[2 + k - 1], AXES, up)  28.5 us
    ppermute x6, starting transfers between devices, on_device(): received_both.append(lax.ppermute(both, AXES, down))  20.9 us
    ppermute x6, starting transfers between devices, on_device(): received_low.append(lax.ppermute(low, AXES, up))  16.9 us
    ppermute x6, starting transfers between devices, on_device(): lax.ppermute(jnp.concatenate([summed[2 + REACH + 2 * (k - 1)], summed[3 +...  13.7 us
    gather x2, local copies, waits for them, and re-layouts, on_device(): key_owner = jnp.take(documents, jnp.maximum(key_place, 0))  9.71 us
    ppermute x6, waiting for transfers between devices, on_device(): grad_low = grad_low + lax.ppermute(summed[2 + k - 1], AXES, up)  6.82 us
    ppermute x6, waiting for transfers between devices, on_device(): received_both.append(lax.ppermute(both, AXES, down))  5.53 us
    unnamed x45, local copies, waits for them, and re-layouts  4.33 us
  transfers between devices with their start and end apart: 24, of which 3 were waited for; matrix products, arithmetic and copies ran while one was open for 17% of the time, Pallas kernels for 0%

profile of v1, /device:TPU:20, one launch (start us, length us, event | category | flops | bytes accessed | tf_op | source)
XLA Modules:
  0.0 151.8 jit_solution(1913452218157279718)
XLA Ops:
  6.2 3.4 %collective-permute-start.1 = (bf16[128,256]{1,0:T(8,128)(2,1)S(1)}, bf16[128,256]{1,0:T(8,128)(2,1)S(1)}, u32[]{:S(2)}, u32[]{:S(2)}) collective-permute-start(bf16[128,256]{1,0:T(8,128)(2,1)S(1)} %get-tuple-element.13), channel_id=1, source_target_pairs={{0,2},{1,3},{2,4},{3,5},{4,6},{5,7},{6,8},{7,9},{8,10},{9,11},{10,... | collective-permute-start | bytes 196616 | tf_op jit(solution)/shard_map/ppermute | solution.py:73
  9.6 4.3 %collective-permute-start.2 = (bf16[128,256]{1,0:T(8,128)(2,1)S(1)}, bf16[128,256]{1,0:T(8,128)(2,1)S(1)}, u32[]{:S(2)}, u32[]{:S(2)}) collective-permute-start(bf16[128,256]{1,0:T(8,128)(2,1)S(1)} %get-tuple-element.13), channel_id=1, source_target_pairs={{0,3},{1,4},{2,5},{3,6},{4,7},{5,8},{6,9},{7,10},{8,11},{9,12},{10... | collective-permute-start | bytes 196616 | tf_op jit(solution)/shard_map/ppermute | solution.py:73
  14.0 3.4 %collective-permute-start.3 = (bf16[128,256]{1,0:T(8,128)(2,1)S(1)}, bf16[128,256]{1,0:T(8,128)(2,1)S(1)}, u32[]{:S(2)}, u32[]{:S(2)}) collective-permute-start(bf16[128,256]{1,0:T(8,128)(2,1)S(1)} %get-tuple-element.13), channel_id=1, source_target_pairs={{0,4},{1,5},{2,6},{3,7},{4,8},{5,9},{6,10},{7,11},{8,12},{9,13},{1... | collective-permute-start | bytes 196616 | tf_op jit(solution)/shard_map/ppermute | solution.py:73
  23.8 9.7 %gather_fusion.1 = s32[1792]{0:T(1024)S(1)} fusion(s32[8192]{0:T(1024)S(1)} %copy-done, s32[2048]{0:T(1024)S(1)} %pad_clamp_fusion), kind=kCustom, calls=%fused_computation.3 | custom fusion | bytes 21504 | tf_op jit(solution)/shard_map/jit(_take)/gather | solution.py:104
  40.9 3.1 %collective-permute-start.6 = (bf16[256,256]{1,0:T(8,128)(2,1)S(1)}, bf16[256,256]{1,0:T(8,128)(2,1)S(1)}, u32[]{:S(2)}, u32[]{:S(2)}) collective-permute-start(bf16[256,256]{1,0:T(8,128)(2,1)S(1)} %pad_maximum_fusion.15), channel_id=1, source_target_pairs={{1,0},{2,1},{3,2},{4,3},{5,4},{6,5},{7,6},{8,7},{9,8},{10,9},{11,1... | collective-permute-start | bytes 393224 | tf_op jit(solution)/shard_map/ppermute | solution.py:74
  44.0 3.7 %collective-permute-start.7 = (bf16[256,256]{1,0:T(8,128)(2,1)S(1)}, bf16[256,256]{1,0:T(8,128)(2,1)S(1)}, u32[]{:S(2)}, u32[]{:S(2)}) collective-permute-start(bf16[256,256]{1,0:T(8,128)(2,1)S(1)} %pad_maximum_fusion.15), channel_id=1, source_target_pairs={{2,0},{3,1},{4,2},{5,3},{6,4},{7,5},{8,6},{9,7},{10,8},{11,9},{12,... | collective-permute-start | bytes 393224 | tf_op jit(solution)/shard_map/ppermute | solution.py:74
  47.7 3.2 %collective-permute-start.8 = (bf16[256,256]{1,0:T(8,128)(2,1)S(1)}, bf16[256,256]{1,0:T(8,128)(2,1)S(1)}, u32[]{:S(2)}, u32[]{:S(2)}) collective-permute-start(bf16[256,256]{1,0:T(8,128)(2,1)S(1)} %pad_maximum_fusion.15), channel_id=1, source_target_pairs={{3,0},{4,1},{5,2},{6,3},{7,4},{8,5},{9,6},{10,7},{11,8},{12,9},{13... | collective-permute-start | bytes 393224 | tf_op jit(solution)/shard_map/ppermute | solution.py:74
  50.9 3.2 %collective-permute-start.9 = (bf16[256,256]{1,0:T(8,128)(2,1)S(1)}, bf16[256,256]{1,0:T(8,128)(2,1)S(1)}, u32[]{:S(2)}, u32[]{:S(2)}) collective-permute-start(bf16[256,256]{1,0:T(8,128)(2,1)S(1)} %pad_maximum_fusion.15), channel_id=1, source_target_pairs={{4,0},{5,1},{6,2},{7,3},{8,4},{9,5},{10,6},{11,7},{12,8},{13,9},{1... | collective-permute-start | bytes 393224 | tf_op jit(solution)/shard_map/ppermute | solution.py:74
  54.2 4.5 %collective-permute-start.10 = (bf16[256,256]{1,0:T(8,128)(2,1)S(1)}, bf16[256,256]{1,0:T(8,128)(2,1)S(1)}, u32[]{:S(2)}, u32[]{:S(2)}) collective-permute-start(bf16[256,256]{1,0:T(8,128)(2,1)S(1)} %pad_maximum_fusion.15), channel_id=1, source_target_pairs={{5,0},{6,1},{7,2},{8,3},{9,4},{10,5},{11,6},{12,7},{13,8},{14,9},{... | collective-permute-start | bytes 393224 | tf_op jit(solution)/shard_map/ppermute | solution.py:74
  58.7 3.3 %collective-permute-start.11 = (bf16[256,256]{1,0:T(8,128)(2,1)S(1)}, bf16[256,256]{1,0:T(8,128)(2,1)S(1)}, u32[]{:S(2)}, u32[]{:S(2)}) collective-permute-start(bf16[256,256]{1,0:T(8,128)(2,1)S(1)} %pad_maximum_fusion.15), channel_id=1, source_target_pairs={{6,0},{7,1},{8,2},{9,3},{10,4},{11,5},{12,6},{13,7},{14,8},{15,9},... | collective-permute-start | bytes 393224 | tf_op jit(solution)/shard_map/ppermute | solution.py:74
  62.2 5.5 %collective-permute-done.11 = bf16[256,256]{1,0:T(8,128)(2,1)S(1)} collective-permute-done((bf16[256,256]{1,0:T(8,128)(2,1)S(1)}, bf16[256,256]{1,0:T(8,128)(2,1)S(1)}, u32[]{:S(2)}, u32[]{:S(2)}) %collective-permute-start.11) | collective-permute-done | bytes 131104 | tf_op jit(solution)/shard_map/ppermute | solution.py:74
  83.8 2.2 %gather_fusion.3 = f32[20,128,256]{2,1,0:T(8,128)} fusion(f32[15,128,256]{2,1,0:T(8,128)S(1)} %concatenate.47, s32[1024]{0:T(1024)S(1)} %get-tuple-element.51), kind=kCustom, calls=%fused_computation.clone | custom fusion | bytes 5242960 | tf_op jit(solution)/shard_map/jit(_take)/gather | solution.py:140
  86.1 2.3 %gather_fusion.4 = f32[20,128,256]{2,1,0:T(8,128)} fusion(f32[15,128,256]{2,1,0:T(8,128)S(1)} %concatenate.47, s32[1024]{0:T(1024)S(1)} %get-tuple-element.50), kind=kCustom, calls=%fused_computation.1.clone | custom fusion | bytes 5242960 | tf_op jit(solution)/shard_map/jit(_take)/gather | solution.py:140
  88.3 3.1 %select_add_fusion = f32[20,128,256]{2,1,0:T(8,128)S(1)} fusion(f32[20,128,256]{2,1,0:T(8,128)} %gather_fusion.4, f32[20,128,256]{2,1,0:T(8,128)} %gather_fusion.3, pred[20]{0:T(512)(128)(4,1)S(1)} %copy-done.8, pred[20]{0:T(512)(128)(4,1)S(1)} %copy-done.7), kind=kLoop, calls=%fused_computation.22 | loop fusion | flops 1966080 | bytes 7864360 | tf_op jit(solution)/shard_map/add | solution.py:140
  95.1 3.1 %collective-permute-start.15 = (f32[256,256]{1,0:T(8,128)}, f32[256,256]{1,0:T(8,128)}, u32[]{:S(2)}, u32[]{:S(2)}) collective-permute-start(f32[256,256]{1,0:T(8,128)} %pad_maximum_fusion.9), channel_id=1, source_target_pairs={{0,2},{1,3},{2,4},{3,5},{4,6},{5,7},{6,8},{7,9},{8,10},{9,11},{10,... | collective-permute-start | bytes 786440 | tf_op jit(solution)/shard_map/ppermute | solution.py:148
  98.9 2.2 %collective-permute-start.17 = (f32[256,256]{1,0:T(8,128)}, f32[256,256]{1,0:T(8,128)}, u32[]{:S(2)}, u32[]{:S(2)}) collective-permute-start(f32[256,256]{1,0:T(8,128)} %pad_maximum_fusion.10), channel_id=1, source_target_pairs={{0,3},{1,4},{2,5},{3,6},{4,7},{5,8},{6,9},{7,10},{8,11},{9,12},{10... | collective-permute-start | bytes 786440 | tf_op jit(solution)/shard_map/ppermute | solution.py:148
  101.8 2.3 %collective-permute-start.19 = (f32[256,256]{1,0:T(8,128)}, f32[256,256]{1,0:T(8,128)}, u32[]{:S(2)}, u32[]{:S(2)}) collective-permute-start(f32[256,256]{1,0:T(8,128)} %pad_maximum_fusion.11), channel_id=1, source_target_pairs={{0,4},{1,5},{2,6},{3,7},{4,8},{5,9},{6,10},{7,11},{8,12},{9,13},{1... | collective-permute-start | bytes 786440 | tf_op jit(solution)/shard_map/ppermute | solution.py:148
  104.2 3.5 %collective-permute-start.12 = (f32[128,256]{1,0:T(8,128)S(1)}, f32[128,256]{1,0:T(8,128)S(1)}, u32[]{:S(2)}, u32[]{:S(2)}) collective-permute-start(f32[128,256]{1,0:T(8,128)S(1)} %get-tuple-element.14), channel_id=1, source_target_pairs={{1,0},{2,1},{3,2},{4,3},{5,4},{6,5},{7,6},{8,7},{9,8},{10,9},{11,1... | collective-permute-start | bytes 393224 | tf_op jit(solution)/shard_map/ppermute | solution.py:147
  110.4 2.2 %collective-permute-start.21 = (f32[256,256]{1,0:T(8,128)}, f32[256,256]{1,0:T(8,128)}, u32[]{:S(2)}, u32[]{:S(2)}) collective-permute-start(f32[256,256]{1,0:T(8,128)} %pad_maximum_fusion.12), channel_id=1, source_target_pairs={{0,5},{1,6},{2,7},{3,8},{4,9},{5,10},{6,11},{7,12},{8,13},{9,14},{... | collective-permute-start | bytes 786440 | tf_op jit(solution)/shard_map/ppermute | solution.py:148
  117.2 5.1 %collective-permute-start.14 = (f32[128,256]{1,0:T(8,128)}, f32[128,256]{1,0:T(8,128)S(1)}, u32[]{:S(2)}, u32[]{:S(2)}) collective-permute-start(f32[128,256]{1,0:T(8,128)} %get-tuple-element.29), channel_id=1, source_target_pairs={{2,0},{3,1},{4,2},{5,3},{6,4},{7,5},{8,6},{9,7},{10,8},{11,9},{12,... | collective-permute-start | bytes 393224 | tf_op jit(solution)/shard_map/ppermute | solution.py:147
  122.3 4.4 %collective-permute-start.16 = (f32[128,256]{1,0:T(8,128)}, f32[128,256]{1,0:T(8,128)S(1)}, u32[]{:S(2)}, u32[]{:S(2)}) collective-permute-start(f32[128,256]{1,0:T(8,128)} %get-tuple-element.26), channel_id=1, source_target_pairs={{3,0},{4,1},{5,2},{6,3},{7,4},{8,5},{9,6},{10,7},{11,8},{12,9},{13... | collective-permute-start | bytes 393224 | tf_op jit(solution)/shard_map/ppermute | solution.py:147
  126.8 3.3 %collective-permute-start.18 = (f32[128,256]{1,0:T(8,128)}, f32[128,256]{1,0:T(8,128)S(1)}, u32[]{:S(2)}, u32[]{:S(2)}) collective-permute-start(f32[128,256]{1,0:T(8,128)} %get-tuple-element.23), channel_id=1, source_target_pairs={{4,0},{5,1},{6,2},{7,3},{8,4},{9,5},{10,6},{11,7},{12,8},{13,9},{1... | collective-permute-start | bytes 393224 | tf_op jit(solution)/shard_map/ppermute | solution.py:147
  130.0 10.2 %collective-permute-start.20 = (f32[128,256]{1,0:T(8,128)}, f32[128,256]{1,0:T(8,128)S(1)}, u32[]{:S(2)}, u32[]{:S(2)}) collective-permute-start(f32[128,256]{1,0:T(8,128)} %get-tuple-element.20), channel_id=1, source_target_pairs={{5,0},{6,1},{7,2},{8,3},{9,4},{10,5},{11,6},{12,7},{13,8},{14,9},{... | collective-permute-start | bytes 393224 | tf_op jit(solution)/shard_map/ppermute | solution.py:147
  143.5 5.6 %collective-permute-done.22 = f32[128,256]{1,0:T(8,128)S(1)} collective-permute-done((f32[128,256]{1,0:T(8,128)}, f32[128,256]{1,0:T(8,128)S(1)}, u32[]{:S(2)}, u32[]{:S(2)}) %collective-permute-start.22) | collective-permute-done | bytes 131104 | tf_op jit(solution)/shard_map/ppermute | solution.py:147
  (138 shorter events, 52.8 us)
Async XLA Ops:
  4.3 34.6 %collective-permute-start = (bf16[128,256]{1,0:T(8,128)(2,1)S(1)}, bf16[128,256]{1,0:T(8,128)(2,1)S(1)}, u32[]{:S(2)}, u32[]{:S(2)}) collective-permute-start(bf16[128,256]{1,0:T(8,128)(2,1)S(1)} %get-tuple-element.13), channel_id=1, source_target_pairs={{0,1},{1,2},{2,3},{3,4},{4,5},{5,6},{6,7},{7,8},{8,9},{9,10},{10,1... | collective-permute-start | bytes 196616 | tf_op jit(solution)/shard_map/ppermute | solution.py:73
  6.2 34.6 %collective-permute-start.1 = (bf16[128,256]{1,0:T(8,128)(2,1)S(1)}, bf16[128,256]{1,0:T(8,128)(2,1)S(1)}, u32[]{:S(2)}, u32[]{:S(2)}) collective-permute-start(bf16[128,256]{1,0:T(8,128)(2,1)S(1)} %get-tuple-element.13), channel_id=1, source_target_pairs={{0,2},{1,3},{2,4},{3,5},{4,6},{5,7},{6,8},{7,9},{8,10},{9,11},{10,... | collective-permute-start | bytes 196616 | tf_op jit(solution)/shard_map/ppermute | solution.py:73
  9.6 34.4 %collective-permute-start.2 = (bf16[128,256]{1,0:T(8,128)(2,1)S(1)}, bf16[128,256]{1,0:T(8,128)(2,1)S(1)}, u32[]{:S(2)}, u32[]{:S(2)}) collective-permute-start(bf16[128,256]{1,0:T(8,128)(2,1)S(1)} %get-tuple-element.13), channel_id=1, source_target_pairs={{0,3},{1,4},{2,5},{3,6},{4,7},{5,8},{6,9},{7,10},{8,11},{9,12},{10... | collective-permute-start | bytes 196616 | tf_op jit(solution)/shard_map/ppermute | solution.py:73
  14.0 33.7 %collective-permute-start.3 = (bf16[128,256]{1,0:T(8,128)(2,1)S(1)}, bf16[128,256]{1,0:T(8,128)(2,1)S(1)}, u32[]{:S(2)}, u32[]{:S(2)}) collective-permute-start(bf16[128,256]{1,0:T(8,128)(2,1)S(1)} %get-tuple-element.13), channel_id=1, source_target_pairs={{0,4},{1,5},{2,6},{3,7},{4,8},{5,9},{6,10},{7,11},{8,12},{9,13},{1... | collective-permute-start | bytes 196616 | tf_op jit(solution)/shard_map/ppermute | solution.py:73
  17.4 33.5 %collective-permute-start.4 = (bf16[128,256]{1,0:T(8,128)(2,1)S(1)}, bf16[128,256]{1,0:T(8,128)(2,1)S(1)}, u32[]{:S(2)}, u32[]{:S(2)}) collective-permute-start(bf16[128,256]{1,0:T(8,128)(2,1)S(1)} %get-tuple-element.13), channel_id=1, source_target_pairs={{0,5},{1,6},{2,7},{3,8},{4,9},{5,10},{6,11},{7,12},{8,13},{9,14},{... | collective-permute-start | bytes 196616 | tf_op jit(solution)/shard_map/ppermute | solution.py:73
  38.9 15.3 %collective-permute-start.5 = (bf16[128,256]{1,0:T(8,128)(2,1)S(1)}, bf16[128,256]{1,0:T(8,128)(2,1)S(1)}, u32[]{:S(2)}, u32[]{:S(2)}) collective-permute-start(bf16[128,256]{1,0:T(8,128)(2,1)S(1)} %get-tuple-element.13), channel_id=1, source_target_pairs={{0,6},{1,7},{2,8},{3,9},{4,10},{5,11},{6,12},{7,13},{8,14},{9,15},... | collective-permute-start | bytes 196616 | tf_op jit(solution)/shard_map/ppermute | solution.py:73
  40.9 17.8 %collective-permute-start.6 = (bf16[256,256]{1,0:T(8,128)(2,1)S(1)}, bf16[256,256]{1,0:T(8,128)(2,1)S(1)}, u32[]{:S(2)}, u32[]{:S(2)}) collective-permute-start(bf16[256,256]{1,0:T(8,128)(2,1)S(1)} %pad_maximum_fusion.15), channel_id=1, source_target_pairs={{1,0},{2,1},{3,2},{4,3},{5,4},{6,5},{7,6},{8,7},{9,8},{10,9},{11,1... | collective-permute-start | bytes 393224 | tf_op jit(solution)/shard_map/ppermute | solution.py:74
  44.0 18.0 %collective-permute-start.7 = (bf16[256,256]{1,0:T(8,128)(2,1)S(1)}, bf16[256,256]{1,0:T(8,128)(2,1)S(1)}, u32[]{:S(2)}, u32[]{:S(2)}) collective-permute-start(bf16[256,256]{1,0:T(8,128)(2,1)S(1)} %pad_maximum_fusion.15), channel_id=1, source_target_pairs={{2,0},{3,1},{4,2},{5,3},{6,4},{7,5},{8,6},{9,7},{10,8},{11,9},{12,... | collective-permute-start | bytes 393224 | tf_op jit(solution)/shard_map/ppermute | solution.py:74
  47.7 14.4 %collective-permute-start.8 = (bf16[256,256]{1,0:T(8,128)(2,1)S(1)}, bf16[256,256]{1,0:T(8,128)(2,1)S(1)}, u32[]{:S(2)}, u32[]{:S(2)}) collective-permute-start(bf16[256,256]{1,0:T(8,128)(2,1)S(1)} %pad_maximum_fusion.15), channel_id=1, source_target_pairs={{3,0},{4,1},{5,2},{6,3},{7,4},{8,5},{9,6},{10,7},{11,8},{12,9},{13... | collective-permute-start | bytes 393224 | tf_op jit(solution)/shard_map/ppermute | solution.py:74
  50.9 11.2 %collective-permute-start.9 = (bf16[256,256]{1,0:T(8,128)(2,1)S(1)}, bf16[256,256]{1,0:T(8,128)(2,1)S(1)}, u32[]{:S(2)}, u32[]{:S(2)}) collective-permute-start(bf16[256,256]{1,0:T(8,128)(2,1)S(1)} %pad_maximum_fusion.15), channel_id=1, source_target_pairs={{4,0},{5,1},{6,2},{7,3},{8,4},{9,5},{10,6},{11,7},{12,8},{13,9},{1... | collective-permute-start | bytes 393224 | tf_op jit(solution)/shard_map/ppermute | solution.py:74
  54.2 7.9 %collective-permute-start.10 = (bf16[256,256]{1,0:T(8,128)(2,1)S(1)}, bf16[256,256]{1,0:T(8,128)(2,1)S(1)}, u32[]{:S(2)}, u32[]{:S(2)}) collective-permute-start(bf16[256,256]{1,0:T(8,128)(2,1)S(1)} %pad_maximum_fusion.15), channel_id=1, source_target_pairs={{5,0},{6,1},{7,2},{8,3},{9,4},{10,5},{11,6},{12,7},{13,8},{14,9},{... | collective-permute-start | bytes 393224 | tf_op jit(solution)/shard_map/ppermute | solution.py:74
  58.7 9.0 %collective-permute-start.11 = (bf16[256,256]{1,0:T(8,128)(2,1)S(1)}, bf16[256,256]{1,0:T(8,128)(2,1)S(1)}, u32[]{:S(2)}, u32[]{:S(2)}) collective-permute-start(bf16[256,256]{1,0:T(8,128)(2,1)S(1)} %pad_maximum_fusion.15), channel_id=1, source_target_pairs={{6,0},{7,1},{8,2},{9,3},{10,4},{11,5},{12,6},{13,7},{14,8},{15,9},... | collective-permute-start | bytes 393224 | tf_op jit(solution)/shard_map/ppermute | solution.py:74
  92.4 20.2 %collective-permute-start.13 = (f32[256,256]{1,0:T(8,128)S(1)}, f32[256,256]{1,0:T(8,128)S(1)}, u32[]{:S(2)}, u32[]{:S(2)}) collective-permute-start(f32[256,256]{1,0:T(8,128)S(1)} %pad_maximum_fusion.8), channel_id=1, source_target_pairs={{0,1},{1,2},{2,3},{3,4},{4,5},{5,6},{6,7},{7,8},{8,9},{9,10},{10,1... | collective-permute-start | bytes 786440 | tf_op jit(solution)/shard_map/ppermute | solution.py:148
  95.1 22.0 %collective-permute-start.15 = (f32[256,256]{1,0:T(8,128)}, f32[256,256]{1,0:T(8,128)}, u32[]{:S(2)}, u32[]{:S(2)}) collective-permute-start(f32[256,256]{1,0:T(8,128)} %pad_maximum_fusion.9), channel_id=1, source_target_pairs={{0,2},{1,3},{2,4},{3,5},{4,6},{5,7},{6,8},{7,9},{8,10},{9,11},{10,... | collective-permute-start | bytes 786440 | tf_op jit(solution)/shard_map/ppermute | solution.py:148
  98.9 23.4 %collective-permute-start.17 = (f32[256,256]{1,0:T(8,128)}, f32[256,256]{1,0:T(8,128)}, u32[]{:S(2)}, u32[]{:S(2)}) collective-permute-start(f32[256,256]{1,0:T(8,128)} %pad_maximum_fusion.10), channel_id=1, source_target_pairs={{0,3},{1,4},{2,5},{3,6},{4,7},{5,8},{6,9},{7,10},{8,11},{9,12},{10... | collective-permute-start | bytes 786440 | tf_op jit(solution)/shard_map/ppermute | solution.py:148
  101.8 24.9 %collective-permute-start.19 = (f32[256,256]{1,0:T(8,128)}, f32[256,256]{1,0:T(8,128)}, u32[]{:S(2)}, u32[]{:S(2)}) collective-permute-start(f32[256,256]{1,0:T(8,128)} %pad_maximum_fusion.11), channel_id=1, source_target_pairs={{0,4},{1,5},{2,6},{3,7},{4,8},{5,9},{6,10},{7,11},{8,12},{9,13},{1... | collective-permute-start | bytes 786440 | tf_op jit(solution)/shard_map/ppermute | solution.py:148
  104.2 6.2 %collective-permute-start.12 = (f32[128,256]{1,0:T(8,128)S(1)}, f32[128,256]{1,0:T(8,128)S(1)}, u32[]{:S(2)}, u32[]{:S(2)}) collective-permute-start(f32[128,256]{1,0:T(8,128)S(1)} %get-tuple-element.14), channel_id=1, source_target_pairs={{1,0},{2,1},{3,2},{4,3},{5,4},{6,5},{7,6},{8,7},{9,8},{10,9},{11,1... | collective-permute-start | bytes 393224 | tf_op jit(solution)/shard_map/ppermute | solution.py:147
  110.4 19.6 %collective-permute-start.21 = (f32[256,256]{1,0:T(8,128)}, f32[256,256]{1,0:T(8,128)}, u32[]{:S(2)}, u32[]{:S(2)}) collective-permute-start(f32[256,256]{1,0:T(8,128)} %pad_maximum_fusion.12), channel_id=1, source_target_pairs={{0,5},{1,6},{2,7},{3,8},{4,9},{5,10},{6,11},{7,12},{8,13},{9,14},{... | collective-permute-start | bytes 786440 | tf_op jit(solution)/shard_map/ppermute | solution.py:148
  113.3 27.0 %collective-permute-start.23 = (f32[256,256]{1,0:T(8,128)}, f32[256,256]{1,0:T(8,128)}, u32[]{:S(2)}, u32[]{:S(2)}) collective-permute-start(f32[256,256]{1,0:T(8,128)} %pad_maximum_fusion.13), channel_id=1, source_target_pairs={{0,6},{1,7},{2,8},{3,9},{4,10},{5,11},{6,12},{7,13},{8,14},{9,15},... | collective-permute-start | bytes 786440 | tf_op jit(solution)/shard_map/ppermute | solution.py:148
  117.2 26.3 %collective-permute-start.14 = (f32[128,256]{1,0:T(8,128)}, f32[128,256]{1,0:T(8,128)S(1)}, u32[]{:S(2)}, u32[]{:S(2)}) collective-permute-start(f32[128,256]{1,0:T(8,128)} %get-tuple-element.29), channel_id=1, source_target_pairs={{2,0},{3,1},{4,2},{5,3},{6,4},{7,5},{8,6},{9,7},{10,8},{11,9},{12,... | collective-permute-start | bytes 393224 | tf_op jit(solution)/shard_map/ppermute | solution.py:147
  122.3 21.1 %collective-permute-start.16 = (f32[128,256]{1,0:T(8,128)}, f32[128,256]{1,0:T(8,128)S(1)}, u32[]{:S(2)}, u32[]{:S(2)}) collective-permute-start(f32[128,256]{1,0:T(8,128)} %get-tuple-element.26), channel_id=1, source_target_pairs={{3,0},{4,1},{5,2},{6,3},{7,4},{8,5},{9,6},{10,7},{11,8},{12,9},{13... | collective-permute-start | bytes 393224 | tf_op jit(solution)/shard_map/ppermute | solution.py:147
  126.8 16.7 %collective-permute-start.18 = (f32[128,256]{1,0:T(8,128)}, f32[128,256]{1,0:T(8,128)S(1)}, u32[]{:S(2)}, u32[]{:S(2)}) collective-permute-start(f32[128,256]{1,0:T(8,128)} %get-tuple-element.23), channel_id=1, source_target_pairs={{4,0},{5,1},{6,2},{7,3},{8,4},{9,5},{10,6},{11,7},{12,8},{13,9},{1... | collective-permute-start | bytes 393224 | tf_op jit(solution)/shard_map/ppermute | solution.py:147
  130.0 13.5 %collective-permute-start.20 = (f32[128,256]{1,0:T(8,128)}, f32[128,256]{1,0:T(8,128)S(1)}, u32[]{:S(2)}, u32[]{:S(2)}) collective-permute-start(f32[128,256]{1,0:T(8,128)} %get-tuple-element.20), channel_id=1, source_target_pairs={{5,0},{6,1},{7,2},{8,3},{9,4},{10,5},{11,6},{12,7},{13,8},{14,9},{... | collective-permute-start | bytes 393224 | tf_op jit(solution)/shard_map/ppermute | solution.py:147
  140.2 8.9 %collective-permute-start.22 = (f32[128,256]{1,0:T(8,128)}, f32[128,256]{1,0:T(8,128)S(1)}, u32[]{:S(2)}, u32[]{:S(2)}) collective-permute-start(f32[128,256]{1,0:T(8,128)} %get-tuple-element.17), channel_id=1, source_target_pairs={{6,0},{7,1},{8,2},{9,3},{10,4},{11,5},{12,6},{13,7},{14,8},{15,9},... | collective-permute-start | bytes 393224 | tf_op jit(solution)/shard_map/ppermute | solution.py:147
  (9 other events, 81.7 us)
